TPU v7x, 128 devices: a whole 4x4x4 slice. The times are simulated.
128 devices in a mesh: row: 8 (over x_lo, z), col: 16 (over y, x_hi, core).
Axes of the slice: x: 4 (x_hi: 2, x_lo: 2; x = x_hi * 2 + x_lo), y: 4, z: 4, core: 2. Of those that a mesh axis runs over, the one named last changes fastest.
Arguments:
- features: bfloat16 [32768, 512], P(('row', 'col')), may hold values from -6 to 6
- cotangent: bfloat16 [32768, 512], P(('row', 'col')), may hold values from -6 to 6
- weights: bfloat16 [512, 512], replicated, may hold values from -0.25 to 0.25
- bias_term: float32 [512], replicated, may hold values from -3 to 3
- adjacency: bfloat16 [8, 16, 128, 128, 128], P('row', 'col'), may hold values from -0.109375 to 0.109375
- tile_rows: int32 [8, 16, 128], P('row', 'col'), may hold values from 0 to 31, as said below
- tile_cols: int32 [8, 16, 128], P('row', 'col'), may hold values from 0 to 15
- tile_count: int32 [8, 16], P('row', 'col'), may hold values from 25 to 128, as said below
Outputs:
- activated: bfloat16 [32768, 512], P(('row', 'col'))
- grad_input: bfloat16 [32768, 512], P(('row', 'col'))
- grad_weight: float32 [512, 512], replicated
- grad_bias: float32 [512], replicated
Inputs may be any that keep to these rules, and one draw needn't show every extreme that they name: Within one device the pairs (tile_rows, tile_cols) over all 128 slots are distinct. Only the first tile_count slots of a device are in use; some device uses all 128.
All inputs are finite; a program needn't handle non-finite values.
Results may differ from a plain program's by a relative error of at most 0.006.
Values may be sent and summed in bfloat16 or wider, within the bound.
No kernel may reach another device: no remote copies, remote signals or barrier semaphores. Data moves between devices by JAX's collectives and lax.ppermute only.
A program may use at most 128 MiB of HBM per device.

v0:
```python
import functools
import math

import jax
import jax.numpy as jnp
from jax import lax
from jax.experimental import pallas as pl
from jax.experimental.pallas import tpu as pltpu
from jax.sharding import PartitionSpec as P


def col_parts(c):
    return c // 4, (c // 2) % 2, c % 2


def relative_col(c2, me):
    y2, x2, k2 = col_parts(c2)
    y1, x1, k1 = col_parts(me)
    return (k2 ^ k1) * 8 + ((y2 - y1) % 4) * 2 + (x2 ^ x1)


def col_send(x, n, move):
    return lax.ppermute(x, "col", [(c, move(c)) for c in range(n)])


def y_up(c):
    return ((c // 4 + 1) % 4) * 4 + c % 4


def y_down(c):
    return ((c // 4 + 3) % 4) * 4 + c % 4


def scatter_sum_col(mine, other, n):
    rest = mine.shape[1:]
    got = col_send(other.reshape((4, 2) + rest), n, lambda c: c ^ 1)
    acc = mine.reshape((4, 2) + rest) + got
    via_up = col_send(acc[2, 0].astype(jnp.bfloat16), n, y_up).astype(jnp.float32)
    via_down = col_send(acc[2, 1].astype(jnp.bfloat16), n, y_down).astype(jnp.float32)
    to_up = jnp.stack([acc[1, 0] + via_up, acc[1, 1]]).astype(jnp.bfloat16)
    to_down = jnp.stack([acc[3, 0], acc[3, 1] + via_down]).astype(jnp.bfloat16)
    total = (
        acc[0]
        + col_send(to_up, n, y_up).astype(jnp.float32)
        + col_send(to_down, n, y_down).astype(jnp.float32)
    )
    return total[0] + col_send(total[1].astype(jnp.bfloat16), n, lambda c: c ^ 2).astype(jnp.float32)


def gather_col(own, n):
    pair = jnp.stack([own, col_send(own, n, lambda c: c ^ 2)])
    from_below = col_send(pair, n, y_up)
    from_above = col_send(pair, n, y_down)
    two_away = jnp.stack([col_send(from_above[0], n, y_down), col_send(from_below[1], n, y_up)])
    quad = jnp.stack([pair, from_above, two_away, from_below])
    rows = (8 * own.shape[0],) + own.shape[1:]
    return quad.reshape(rows), col_send(quad, n, lambda c: c ^ 1).reshape(rows)


def place_kernel(row_offset, slot_ref, adj_ref, dense_ref, dense_t_ref):
    row = pl.program_id(0) + row_offset
    col_total = dense_ref.shape[1] // adj_ref.shape[-1]
    size = adj_ref.shape[-1]
    for col in range(col_total):
        slot = slot_ref[row * col_total + col]
        tile = adj_ref[jnp.maximum(slot, 0)]
        tile = jnp.where(slot >= 0, tile, jnp.zeros_like(tile))
        dense_ref[:, col * size : (col + 1) * size] = tile
        dense_t_ref[col * size : (col + 1) * size, :] = tile.T


def place_rows(slot_of, tile_data, row_offset, row_count, col_total):
    slot_total, size, _ = tile_data.shape
    return pl.pallas_call(
        functools.partial(place_kernel, row_offset),
        grid_spec=pltpu.PrefetchScalarGridSpec(
            num_scalar_prefetch=1,
            grid=(row_count,),
            in_specs=[pl.BlockSpec((slot_total, size, size), lambda r, slots: (0, 0, 0))],
            out_specs=[
                pl.BlockSpec((size, col_total * size), lambda r, slots: (r, 0)),
                pl.BlockSpec((col_total * size, size), lambda r, slots: (0, r)),
            ],
        ),
        out_shape=[
            jax.ShapeDtypeStruct((row_count * size, col_total * size), tile_data.dtype),
            jax.ShapeDtypeStruct((col_total * size, row_count * size), tile_data.dtype),
        ],
        compiler_params=pltpu.CompilerParams(vmem_limit_bytes=48 * 1024 * 1024),
        cost_estimate=pl.CostEstimate(
            flops=0,
            transcendentals=0,
            bytes_accessed=slot_total * size * size * 2 + 2 * row_count * col_total * size * size * 2,
        ),
    )(slot_of, tile_data)


def dense_blocks(tile_data, row_ids, col_ids, in_count, row_total, col_total):
    slot_total = tile_data.shape[0]
    slot_range = jnp.arange(slot_total, dtype=jnp.int32)
    pair_of = jnp.where(slot_range < in_count, row_ids * col_total + col_ids, -1)
    pair_range = jnp.arange(row_total * col_total, dtype=jnp.int32)
    slot_of = jnp.max(
        jnp.where(pair_range[:, None] == pair_of[None, :], slot_range[None, :], -1), axis=1
    )
    half = row_total // 2
    mine, mine_t = place_rows(slot_of, tile_data, 0, half, col_total)
    other, other_t = place_rows(slot_of, tile_data, half, half, col_total)
    return mine, other, mine_t, other_t


def gather_by_a2a(x, axis_name, n):
    spread = jnp.broadcast_to(x[None], (n,) + x.shape)
    return lax.all_to_all(spread, axis_name, 0, 0, tiled=False).reshape((n * x.shape[0],) + x.shape[1:])


def scatter_sum_by_a2a(x, axis_name, n, link_dtype):
    parts = x.astype(link_dtype).reshape((n, x.shape[0] // n) + x.shape[1:])
    got = lax.all_to_all(parts, axis_name, 0, 0, tiled=False)
    return jnp.sum(got.astype(jnp.float32), axis=0)


def all_sum_by_a2a(x, axis_names, n, scale):
    pad = (-x.shape[0]) % n
    parts = jnp.pad(x, (0, pad)).reshape(n, -1)
    got = lax.all_to_all(parts.astype(jnp.bfloat16), axis_names, 0, 0, tiled=False)
    mine = jnp.sum(got.astype(jnp.float32), axis=0) * scale
    back = lax.all_to_all(jnp.broadcast_to(mine[None], parts.shape), axis_names, 0, 0, tiled=False)
    return back.reshape(-1)[: x.shape[0]]


def slope_of(shifted, cotangent):
    sig = jax.nn.sigmoid(shifted)
    return (cotangent.astype(jnp.float32) * sig * (1.0 + shifted * (1.0 - sig))).astype(
        jnp.bfloat16
    )


def on_device_body(features, cotangent, weights, bias_term, adjacency, tile_rows, tile_cols, tile_count):
    tile_size = adjacency.shape[-1]
    slot_total = adjacency.shape[2]
    tile_data = adjacency.reshape(slot_total, tile_size, tile_size)
    row_ids = tile_rows.reshape(slot_total)
    col_ids = tile_cols.reshape(slot_total)
    in_count = tile_count.reshape(())
    n_row = lax.axis_size("row")
    n_col = lax.axis_size("col")
    own_rows = features.shape[0]
    own_blocks = own_rows // tile_size
    feat_width = features.shape[1]
    row_total = n_col * own_blocks
    col_total = n_row * own_blocks
    node_scale = 1.0 / math.sqrt(own_rows * n_row * n_col)

    me_col = lax.axis_index("col")
    rel_rows = relative_col(row_ids // own_blocks, me_col) * own_blocks + row_ids % own_blocks
    dense_mine, dense_other, dense_t_mine, dense_t_other = dense_blocks(tile_data, rel_rows, col_ids, in_count, row_total, col_total)

    projected = jnp.dot(features, weights, preferred_element_type=jnp.float32).astype(jnp.bfloat16)
    gathered = gather_by_a2a(projected, "row", n_row)
    other_rows = jnp.dot(dense_other, gathered, preferred_element_type=jnp.float32)
    mine_rows = lax.optimization_barrier(
        jnp.dot(dense_mine, gathered, preferred_element_type=jnp.float32)
    )
    bias_row = bias_term[None, :]
    shifted = (
        scatter_sum_col(
            mine_rows.reshape(n_col // 2, own_rows, feat_width),
            other_rows.reshape(n_col // 2, own_rows, feat_width),
            n_col,
        )
        + bias_row
    )
    slope_own = slope_of(shifted, cotangent)
    slope_mine, slope_other = gather_col(slope_own, n_col)
    activated = jax.nn.silu(shifted).astype(jnp.bfloat16)
    bias_part = jnp.sum(slope_own.astype(jnp.float32), axis=0)
    cols_mine = lax.optimization_barrier(
        jnp.dot(dense_t_mine, slope_mine, preferred_element_type=jnp.float32)
    )
    partial_cols = cols_mine + jnp.dot(dense_t_other, slope_other, preferred_element_type=jnp.float32)
    back = scatter_sum_by_a2a(partial_cols, "row", n_row, jnp.bfloat16).astype(jnp.bfloat16)
    grad_input = lax.dot_general(
        back, weights, (((1,), (1,)), ((), ())), preferred_element_type=jnp.float32
    ).astype(jnp.bfloat16)
    weight_part = lax.dot_general(
        features, back, (((0,), (0,)), ((), ())), preferred_element_type=jnp.float32
    )
    joined = jnp.concatenate([weight_part.reshape(-1), bias_part])
    joined = all_sum_by_a2a(joined, ("row", "col"), n_row * n_col, node_scale)
    weight_sum = joined[: feat_width * feat_width].reshape(feat_width, feat_width)
    bias_sum = joined[feat_width * feat_width :]
    return (activated, grad_input, weight_sum, bias_sum)


def solution(mesh):
    return sharded(mesh)


def sharded(mesh):
    return jax.shard_map(
        on_device_body,
        mesh=mesh,
        in_specs=(
            P(("row", "col"), None),
            P(("row", "col"), None),
            P(),
            P(),
            P("row", "col", None, None, None),
            P("row", "col", None),
            P("row", "col", None),
            P("row", "col"),
        ),
        out_specs=(P(("row", "col"), None), P(("row", "col"), None), P(), P()),
        check_vma=False,
    )
```

profile of v0, /device:TPU:1, one launch (start us, length us, event | category | flops | bytes accessed | tf_op | source)
XLA Modules:
  0.0 231.2 jit_solution(13285513569388245124)
XLA Ops:
  0.6 1.0 copy-done
  1.7 1.2 convolution_convert_fusion.2
  2.9 1.5 broadcast_in_dim.20
  4.4 6.9 %all-to-all-start = ((bf16[8,256,512]{2,1,0:T(8,128)(2,1)}), bf16[8,256,512]{2,1,0:T(8,128)(2,1)S(1)}, u32[]{:S(2)}, u32[]{:S(2)}) async-start(bf16[8,256,512]{2,1,0:T(8,128)(2,1)} %broadcast_in_dim.20), calls=%async_computation | async-start | bytes 4194304 | tf_op jit(solution)/shard_map/all_to_all | solution.py:114
  12.1 0.1 select_reduce_fusion.slot_ref
  12.2 2.2 copy-done.1
  14.4 10.5 %shard_map.112 = (bf16[2048,2048]{1,0:T(8,128)(2,1)}, bf16[2048,2048]{1,0:T(8,128)(2,1)}) custom-call(s32[512]{0:T(512)S(1)} %select_reduce_fusion.slot_ref, bf16[128,128,128]{2,1,0:T(8,128)(2,1)S(1)} %bitcast.109), custom_call_target="tpu_custom_call" | custom-call | bytes 20971520 | tf_op jit(solution)/shard_map/pallas_call | solution.py:74
  24.9 12.6 %all-to-all-done = bf16[8,256,512]{2,1,0:T(8,128)(2,1)S(1)} async-done(((bf16[8,256,512]{2,1,0:T(8,128)(2,1)}), bf16[8,256,512]{2,1,0:T(8,128)(2,1)S(1)}, u32[]{:S(2)}, u32[]{:S(2)}) %all-to-all-start) | async-done | bytes 2097184 | tf_op jit(solution)/shard_map/all_to_all | solution.py:114
  37.6 7.0 %fusion.25 = f32[4,2,256,512]{3,2,1,0:T(8,128)S(1)} fusion(bf16[4,2,256,2048]{3,2,1,0:T(8,128)(2,1)} %bitcast.128, bf16[2048,512,1,1]{1,0,3,2:T(8,128)(2,1)S(1)} %bitcast.113), kind=kOutput, calls=%fused_computation.75 | convolution fusion | flops 4294967296 | bytes 14680064 | tf_op jit(solution)/shard_map/dot_general | solution.py:161
  44.6 0.9 collective-permute-start
  45.5 10.5 %shard_map.111 = (bf16[2048,2048]{1,0:T(8,128)(2,1)}, bf16[2048,2048]{1,0:T(8,128)(2,1)}) custom-call(s32[512]{0:T(512)S(1)} %select_reduce_fusion.slot_ref, bf16[128,128,128]{2,1,0:T(8,128)(2,1)S(1)} %bitcast.110), custom_call_target="tpu_custom_call" | custom-call | bytes 20971520 | tf_op jit(solution)/shard_map/pallas_call | solution.py:74
  56.0 6.9 %fusion.24 = f32[2048,512]{1,0:T(8,128)S(1)} fusion(bf16[2048,2048]{1,0:T(8,128)(2,1)} %get-tuple-element.8, bf16[2048,512]{1,0:T(8,128)(2,1)S(1)} %bitcast.114), kind=kOutput, calls=%fused_computation.74 | convolution fusion | flops 4294967296 | bytes 14680064 | tf_op jit(solution)/shard_map/dot_general | solution.py:163
  62.9 1.1 fusion.23
  63.9 0.1 slice_bitcast_fusion.9
  64.0 1.4 collective-permute-start.1
  65.4 1.5 collective-permute-start.3
  66.9 6.4 %collective-permute-done.1 = bf16[256,512]{1,0:T(8,128)(2,1)S(1)} collective-permute-done((bf16[256,512]{1,0:T(8,128)(2,1)S(1)}, bf16[256,512]{1,0:T(8,128)(2,1)S(1)}, u32[]{:S(2)}, u32[]{:S(2)}) %collective-permute-start.1) | collective-permute-done | bytes 262176 | tf_op jit(solution)/shard_map/ppermute | solution.py:23
  73.2 0.2 fusion.9
  73.4 0.1 pad_maximum_fusion.2
  73.5 1.0 collective-permute-start.2
  74.5 0.1 pad_maximum_fusion.3
  74.6 1.8 collective-permute-start.4
  76.4 11.0 %collective-permute-done.2 = bf16[2,256,512]{2,1,0:T(8,128)(2,1)S(1)} collective-permute-done((bf16[2,256,512]{2,1,0:T(8,128)(2,1)S(1)}, bf16[2,256,512]{2,1,0:T(8,128)(2,1)S(1)}, u32[]{:S(2)}, u32[]{:S(2)}) %collective-permute-start.2) | collective-permute-done | bytes 524320 | tf_op jit(solution)/shard_map/ppermute | solution.py:23
  87.4 0.2 fusion.2
  87.7 2.6 %collective-permute-start.5 = (bf16[256,512]{1,0:T(8,128)(2,1)S(1)}, bf16[256,512]{1,0:T(8,128)(2,1)S(1)}, u32[]{:S(2)}, u32[]{:S(2)}) collective-permute-start(bf16[256,512]{1,0:T(8,128)(2,1)S(1)} %fusion.11), channel_id=1, source_target_pairs={{0,2},{1,3},{2,0},{3,1},{4,6},{5,7},{6,4},{7,5},{8,10},{9,11},{10,... | collective-permute-start | bytes 786440 | tf_op jit(solution)/shard_map/ppermute | solution.py:23
  90.3 5.1 %collective-permute-done.5 = bf16[256,512]{1,0:T(8,128)(2,1)S(1)} collective-permute-done((bf16[256,512]{1,0:T(8,128)(2,1)S(1)}, bf16[256,512]{1,0:T(8,128)(2,1)S(1)}, u32[]{:S(2)}, u32[]{:S(2)}) %collective-permute-start.5) | collective-permute-done | bytes 262176 | tf_op jit(solution)/shard_map/ppermute | solution.py:23
  95.4 0.3 fusion.22
  95.7 2.6 %collective-permute-start.6 = (bf16[256,512]{1,0:T(8,128)(2,1)S(1)}, bf16[256,512]{1,0:T(8,128)(2,1)S(1)}, u32[]{:S(2)}, u32[]{:S(2)}) collective-permute-start(bf16[256,512]{1,0:T(8,128)(2,1)S(1)} %get-tuple-element.13), channel_id=1, source_target_pairs={{0,2},{1,3},{2,0},{3,1},{4,6},{5,7},{6,4},{7,5},{8,10},{9,11},{10,... | collective-permute-start | bytes 786440 | tf_op jit(solution)/shard_map/ppermute | solution.py:23
  98.3 4.2 %collective-permute-done.6 = bf16[256,512]{1,0:T(8,128)(2,1)S(1)} collective-permute-done((bf16[256,512]{1,0:T(8,128)(2,1)S(1)}, bf16[256,512]{1,0:T(8,128)(2,1)S(1)}, u32[]{:S(2)}, u32[]{:S(2)}) %collective-permute-start.6) | collective-permute-done | bytes 262176 | tf_op jit(solution)/shard_map/ppermute | solution.py:23
  102.5 0.1 fusion.21
  102.6 2.3 %collective-permute-start.7 = (bf16[2,256,512]{2,1,0:T(8,128)(2,1)S(1)}, bf16[2,256,512]{2,1,0:T(8,128)(2,1)S(1)}, u32[]{:S(2)}, u32[]{:S(2)}) collective-permute-start(bf16[2,256,512]{2,1,0:T(8,128)(2,1)S(1)} %get-tuple-element.23), channel_id=1, source_target_pairs={{0,12},{1,13},{2,14},{3,15},{4,0},{5,1},{6,2},{7,3},{8,4},{9,5},{1... | collective-permute-start | bytes 1572872 | tf_op jit(solution)/shard_map/ppermute | solution.py:23
  104.9 7.5 %collective-permute-done.7 = bf16[2,256,512]{2,1,0:T(8,128)(2,1)S(1)} collective-permute-done((bf16[2,256,512]{2,1,0:T(8,128)(2,1)S(1)}, bf16[2,256,512]{2,1,0:T(8,128)(2,1)S(1)}, u32[]{:S(2)}, u32[]{:S(2)}) %collective-permute-start.7) | collective-permute-done | bytes 524320 | tf_op jit(solution)/shard_map/ppermute | solution.py:23
  112.4 3.3 %collective-permute-start.8 = (bf16[256,512]{1,0:T(8,128)(2,1)S(1)}, bf16[256,512]{1,0:T(8,128)(2,1)S(1)}, u32[]{:S(2)}, u32[]{:S(2)}) collective-permute-start(bf16[256,512]{1,0:T(8,128)(2,1)S(1)} %slice_bitcast_fusion.5), channel_id=1, source_target_pairs={{0,12},{1,13},{2,14},{3,15},{4,0},{5,1},{6,2},{7,3},{8,4},{9,5},{1... | collective-permute-start | bytes 786440 | tf_op jit(solution)/shard_map/ppermute | solution.py:23
  115.7 0.1 collective-permute-start.10
  115.8 3.6 %collective-permute-done.8 = bf16[256,512]{1,0:T(8,128)(2,1)S(1)} collective-permute-done((bf16[256,512]{1,0:T(8,128)(2,1)S(1)}, bf16[256,512]{1,0:T(8,128)(2,1)S(1)}, u32[]{:S(2)}, u32[]{:S(2)}) %collective-permute-start.8) | collective-permute-done | bytes 262176 | tf_op jit(solution)/shard_map/ppermute | solution.py:23
  119.4 3.1 %collective-permute-done.10 = bf16[256,512]{1,0:T(8,128)(2,1)S(1)} collective-permute-done((bf16[256,512]{1,0:T(8,128)(2,1)S(1)}, bf16[256,512]{1,0:T(8,128)(2,1)S(1)}, u32[]{:S(2)}, u32[]{:S(2)}) %collective-permute-start.10) | collective-permute-done | bytes 262176 | tf_op jit(solution)/shard_map/ppermute | solution.py:23
  122.6 0.1 maximum_bitcast_fusion
  122.6 0.3 pad_maximum_fusion
  122.9 6.6 %collective-permute-start.11 = (bf16[4,2,256,512]{3,2,1,0:T(8,128)(2,1)S(1)}, bf16[4,2,256,512]{3,2,1,0:T(8,128)(2,1)S(1)}, u32[]{:S(2)}, u32[]{:S(2)}) collective-permute-start(bf16[4,2,256,512]{3,2,1,0:T(8,128)(2,1)S(1)} %pad_maximum_fusion), channel_id=1, source_target_pairs={{0,1},{1,0},{2,3},{3,2},{4,5},{5,4},{6,7},{7,6},{8,9},{9,8},{10,11... | collective-permute-start | bytes 6291464 | tf_op jit(solution)/shard_map/ppermute | solution.py:23
  129.6 4.5 %fusion.26 = f32[2048,512]{1,0:T(8,128)S(1)} fusion(bf16[2048,2048]{1,0:T(8,128)(2,1)S(1)} %bitcast.127, bf16[2048,512]{1,0:T(8,128)(2,1)S(1)} %bitcast.115), kind=kOutput, calls=%fused_computation.76 | convolution fusion | flops 4294967296 | bytes 14680064 | tf_op jit(solution)/shard_map/dot_general | solution.py:179
  134.1 4.7 %add_convert_fusion = bf16[2048,512]{1,0:T(8,128)(2,1)S(1)} fusion(f32[2048,512]{1,0:T(8,128)S(1)} %fusion.26, bf16[2048,2048]{1,0:T(8,128)(2,1)S(1)} %bitcast.125, bf16[2048,512]{1,0:T(8,128)(2,1)S(1)} %bitcast.129), kind=kOutput, calls=%fused_computation | convolution fusion | flops 4297064448 | bytes 16777216 | tf_op jit(solution)/shard_map/dot_general | solution.py:181
  138.8 28.9 %all_to_all.22 = bf16[8,256,512]{2,1,0:T(8,128)(2,1)S(1)} all-to-all(bf16[8,256,512]{2,1,0:T(8,128)(2,1)S(1)} %bitcast.116), channel_id=1, replica_groups=mesh['row'=8,'col'=16] {'row'}, dimensions={0} | all-to-all | bytes 4194304 | tf_op jit(solution)/shard_map/all_to_all | solution.py:119
  167.7 0.4 reduce_sum.30
  168.1 0.6 copy-done.5
  168.6 0.3 fusion
  168.9 0.2 copy.15
  169.2 0.2 copy.18
  169.4 0.6 convert_element_type.84
  170.0 0.5 broadcast.233
  170.5 4.3 %reduce.6 = bf16[128,2052]{1,0:T(8,128)(2,1)S(1)} reduce(bf16[128,1,2052]{2,1,0:T(2,128)(2,1)S(1)} %convert_element_type.84, bf16[]{:T(256)} %broadcast.233), dimensions={1}, to_apply=%convert_element_type.84.reduce_sub_computation | reduce | bytes 1050626 | tf_op jit(solution)/shard_map/convert_element_type | solution.py:126
  174.9 0.6 reshape.212
  175.4 20.4 %all_to_all.23 = bf16[128,2,1026]{2,1,0:T(2,128)(2,1)S(1)} all-to-all(bf16[128,2,1026]{2,1,0:T(2,128)(2,1)S(1)} %reshape.212), channel_id=1, replica_groups=mesh['row'=8,'col'=16] {'row','col'}, dimensions={0} | all-to-all | bytes 1050624 | tf_op jit(solution)/shard_map/all_to_all | solution.py:126
  195.9 0.7 reshape.213
  196.6 1.2 convert_reduce_fusion
  197.8 1.6 broadcast_in_dim.21
  199.4 4.0 %all-to-all-start.3 = ((f32[128,1,2052]{2,1,0:T(1,128)}), f32[128,1,2052]{2,1,0:T(1,128)S(1)}, u32[]{:S(2)}, u32[]{:S(2)}) async-start(f32[128,1,2052]{2,1,0:T(1,128)} %broadcast_in_dim.21), calls=%async_computation.3 | async-start | bytes 2228224 | tf_op jit(solution)/shard_map/all_to_all | solution.py:128
  203.4 0.9 multiply_convert_fusion.1
  204.3 1.0 convolution_convert_fusion.1
  205.3 18.0 %all-to-all-done.3 = f32[128,1,2052]{2,1,0:T(1,128)S(1)} async-done(((f32[128,1,2052]{2,1,0:T(1,128)}), f32[128,1,2052]{2,1,0:T(1,128)S(1)}, u32[]{:S(2)}, u32[]{:S(2)}) %all-to-all-start.3) | async-done | bytes 1050656 | tf_op jit(solution)/shard_map/all_to_all | solution.py:128
  223.3 2.7 %reduce.3 = f32[128,2052]{1,0:T(8,128)S(1)} reduce(f32[128,1,2052]{2,1,0:T(1,128)S(1)} %all-to-all-done.3, f32[]{:T(128)} %constant.116), dimensions={1}, to_apply=%all_to_all.17.reduce_sub_computation | reduce | bytes 2101252 | tf_op jit(solution)/shard_map/all_to_all | solution.py:128
  226.0 1.1 slice.58
  227.1 1.8 reshape.208
  228.9 1.0 slice.72
  229.9 1.3 slice.73
  (43 shorter events, 0.2 us)
Async XLA Ops:
  0.6 1.0 copy-start
  4.4 7.6 %copy-start.10 = (s32[1,1,128]{2,1,0:T(1,128)S(1)}, s32[1,1,128]{2,1,0:T(1,128)}, u32[]{:S(2)}) copy-start(s32[1,1,128]{2,1,0:T(1,128)} %param.14) | copy-start | bytes 1540
  4.4 7.6 %copy-start.11 = (s32[1,1,128]{2,1,0:T(1,128)S(1)}, s32[1,1,128]{2,1,0:T(1,128)}, u32[]{:S(2)}) copy-start(s32[1,1,128]{2,1,0:T(1,128)} %param.13) | copy-start | bytes 1540
  4.4 33.1 %all-to-all-start = ((bf16[8,256,512]{2,1,0:T(8,128)(2,1)}), bf16[8,256,512]{2,1,0:T(8,128)(2,1)S(1)}, u32[]{:S(2)}, u32[]{:S(2)}) async-start(bf16[8,256,512]{2,1,0:T(8,128)(2,1)} %broadcast_in_dim.20), calls=%async_computation | async-start | bytes 4194304 | tf_op jit(solution)/shard_map/all_to_all | solution.py:114
  12.2 2.2 copy-start.1
  37.6 7.9 %copy-start.2 = (bf16[1,1,128,128,128]{4,3,2,1,0:T(8,128)(2,1)S(1)}, bf16[1,1,128,128,128]{4,3,2,1,0:T(8,128)(2,1)}, u32[]{:S(2)}) copy-start(bf16[1,1,128,128,128]{4,3,2,1,0:T(8,128)(2,1)} %param.12) | copy-start | bytes 12582916
  44.6 18.3 %collective-permute-start = (f32[4,2,256,512]{3,2,1,0:T(8,128)S(1)}, f32[4,2,256,512]{3,2,1,0:T(8,128)S(1)}, u32[]{:S(2)}, u32[]{:S(2)}) collective-permute-start(f32[4,2,256,512]{3,2,1,0:T(8,128)S(1)} %fusion.25), channel_id=1, source_target_pairs={{0,1},{1,0},{2,3},{3,2},{4,5},{5,4},{6,7},{7,6},{8,9},{9,8},{10,11... | collective-permute-start | bytes 12582920 | tf_op jit(solution)/shard_map/ppermute | solution.py:23
  64.0 9.2 %collective-permute-start.1 = (bf16[256,512]{1,0:T(8,128)(2,1)S(1)}, bf16[256,512]{1,0:T(8,128)(2,1)S(1)}, u32[]{:S(2)}, u32[]{:S(2)}) collective-permute-start(bf16[256,512]{1,0:T(8,128)(2,1)S(1)} %get-tuple-element.18), channel_id=1, source_target_pairs={{0,4},{1,5},{2,6},{3,7},{4,8},{5,9},{6,10},{7,11},{8,12},{9,13},{1... | collective-permute-start | bytes 786440 | tf_op jit(solution)/shard_map/ppermute | solution.py:23
  65.4 7.9 %collective-permute-start.3 = (bf16[256,512]{1,0:T(8,128)(2,1)S(1)}, bf16[256,512]{1,0:T(8,128)(2,1)S(1)}, u32[]{:S(2)}, u32[]{:S(2)}) collective-permute-start(bf16[256,512]{1,0:T(8,128)(2,1)S(1)} %get-tuple-element.19), channel_id=1, source_target_pairs={{0,12},{1,13},{2,14},{3,15},{4,0},{5,1},{6,2},{7,3},{8,4},{9,5},{1... | collective-permute-start | bytes 786440 | tf_op jit(solution)/shard_map/ppermute | solution.py:23
  73.2 56.3 %slice-start.2 = ((s8[8388608]{0:T(1024)(128)(4,1)}), s8[4194304]{0:T(1024)(128)(4,1)S(1)}, s32[]{:S(2)}) async-start(s8[8388608]{0:T(1024)(128)(4,1)} %bitcast.126), calls=%async_computation.6 | async-start | bytes 8388608
  73.5 13.9 %collective-permute-start.2 = (bf16[2,256,512]{2,1,0:T(8,128)(2,1)S(1)}, bf16[2,256,512]{2,1,0:T(8,128)(2,1)S(1)}, u32[]{:S(2)}, u32[]{:S(2)}) collective-permute-start(bf16[2,256,512]{2,1,0:T(8,128)(2,1)S(1)} %pad_maximum_fusion.2), channel_id=1, source_target_pairs={{0,4},{1,5},{2,6},{3,7},{4,8},{5,9},{6,10},{7,11},{8,12},{9,13},{1... | collective-permute-start | bytes 1572872 | tf_op jit(solution)/shard_map/ppermute | solution.py:23
  74.6 20.8 %copy-start.8 = (bf16[256,512]{1,0:T(8,128)(2,1)S(1)}, bf16[256,512]{1,0:T(8,128)(2,1)}, u32[]{:S(2)}) copy-start(bf16[256,512]{1,0:T(8,128)(2,1)} %param.9) | copy-start | bytes 786436
  74.6 20.8 %copy-start.9 = (f32[512]{0:T(512)S(1)}, f32[512]{0:T(512)}, u32[]{:S(2)}) copy-start(f32[512]{0:T(512)} %param.11) | copy-start | bytes 6148
  74.6 12.8 %collective-permute-start.4 = (bf16[2,256,512]{2,1,0:T(8,128)(2,1)S(1)}, bf16[2,256,512]{2,1,0:T(8,128)(2,1)S(1)}, u32[]{:S(2)}, u32[]{:S(2)}) collective-permute-start(bf16[2,256,512]{2,1,0:T(8,128)(2,1)S(1)} %pad_maximum_fusion.3), channel_id=1, source_target_pairs={{0,12},{1,13},{2,14},{3,15},{4,0},{5,1},{6,2},{7,3},{8,4},{9,5},{1... | collective-permute-start | bytes 1572872 | tf_op jit(solution)/shard_map/ppermute | solution.py:23
  87.6 28.1 %copy-start.3 = (f32[2,256,512]{2,1,0:T(8,128)}, f32[2,256,512]{2,1,0:T(8,128)S(1)}, u32[]{:S(2)}) copy-start(f32[2,256,512]{2,1,0:T(8,128)S(1)} %fusion.2) | copy-start | bytes 3145732
  87.6 41.9 %slice-start.3 = ((s8[8388608]{0:T(1024)(128)(4,1)}), s8[4194304]{0:T(1024)(128)(4,1)S(1)}, s32[]{:S(2)}) async-start(s8[8388608]{0:T(1024)(128)(4,1)} %bitcast.126), calls=%async_computation.7 | async-start | bytes 8388608
  87.7 7.7 %collective-permute-start.5 = (bf16[256,512]{1,0:T(8,128)(2,1)S(1)}, bf16[256,512]{1,0:T(8,128)(2,1)S(1)}, u32[]{:S(2)}, u32[]{:S(2)}) collective-permute-start(bf16[256,512]{1,0:T(8,128)(2,1)S(1)} %fusion.11), channel_id=1, source_target_pairs={{0,2},{1,3},{2,0},{3,1},{4,6},{5,7},{6,4},{7,5},{8,10},{9,11},{10,... | collective-permute-start | bytes 786440 | tf_op jit(solution)/shard_map/ppermute | solution.py:23
  95.4 27.2 %copy-start.6 = (bf16[256,512]{1,0:T(8,128)(2,1)}, bf16[256,512]{1,0:T(8,128)(2,1)S(1)}, u32[]{:S(2)}) copy-start(bf16[256,512]{1,0:T(8,128)(2,1)S(1)} %collective-permute-done.5) | copy-start | bytes 786436
  95.7 6.8 %collective-permute-start.6 = (bf16[256,512]{1,0:T(8,128)(2,1)S(1)}, bf16[256,512]{1,0:T(8,128)(2,1)S(1)}, u32[]{:S(2)}, u32[]{:S(2)}) collective-permute-start(bf16[256,512]{1,0:T(8,128)(2,1)S(1)} %get-tuple-element.13), channel_id=1, source_target_pairs={{0,2},{1,3},{2,0},{3,1},{4,6},{5,7},{6,4},{7,5},{8,10},{9,11},{10,... | collective-permute-start | bytes 786440 | tf_op jit(solution)/shard_map/ppermute | solution.py:23
  102.6 9.8 %collective-permute-start.7 = (bf16[2,256,512]{2,1,0:T(8,128)(2,1)S(1)}, bf16[2,256,512]{2,1,0:T(8,128)(2,1)S(1)}, u32[]{:S(2)}, u32[]{:S(2)}) collective-permute-start(bf16[2,256,512]{2,1,0:T(8,128)(2,1)S(1)} %get-tuple-element.23), channel_id=1, source_target_pairs={{0,12},{1,13},{2,14},{3,15},{4,0},{5,1},{6,2},{7,3},{8,4},{9,5},{1... | collective-permute-start | bytes 1572872 | tf_op jit(solution)/shard_map/ppermute | solution.py:23
  104.9 10.8 %collective-permute-start.9 = (bf16[2,256,512]{2,1,0:T(8,128)(2,1)S(1)}, bf16[2,256,512]{2,1,0:T(8,128)(2,1)S(1)}, u32[]{:S(2)}, u32[]{:S(2)}) collective-permute-start(bf16[2,256,512]{2,1,0:T(8,128)(2,1)S(1)} %get-tuple-element.23), channel_id=1, source_target_pairs={{0,4},{1,5},{2,6},{3,7},{4,8},{5,9},{6,10},{7,11},{8,12},{9,13},{1... | collective-permute-start | bytes 1572872 | tf_op jit(solution)/shard_map/ppermute | solution.py:23
  112.4 7.0 %collective-permute-start.8 = (bf16[256,512]{1,0:T(8,128)(2,1)S(1)}, bf16[256,512]{1,0:T(8,128)(2,1)S(1)}, u32[]{:S(2)}, u32[]{:S(2)}) collective-permute-start(bf16[256,512]{1,0:T(8,128)(2,1)S(1)} %slice_bitcast_fusion.5), channel_id=1, source_target_pairs={{0,12},{1,13},{2,14},{3,15},{4,0},{5,1},{6,2},{7,3},{8,4},{9,5},{1... | collective-permute-start | bytes 786440 | tf_op jit(solution)/shard_map/ppermute | solution.py:23
  115.7 6.8 %collective-permute-start.10 = (bf16[256,512]{1,0:T(8,128)(2,1)S(1)}, bf16[256,512]{1,0:T(8,128)(2,1)S(1)}, u32[]{:S(2)}, u32[]{:S(2)}) collective-permute-start(bf16[256,512]{1,0:T(8,128)(2,1)S(1)} %slice_bitcast_fusion.4), channel_id=1, source_target_pairs={{0,4},{1,5},{2,6},{3,7},{4,8},{5,9},{6,10},{7,11},{8,12},{9,13},{1... | collective-permute-start | bytes 786440 | tf_op jit(solution)/shard_map/ppermute | solution.py:23
  122.6 11.5 %slice-start = ((s8[8388608]{0:T(1024)(128)(4,1)}), s8[4194304]{0:T(1024)(128)(4,1)S(1)}, s32[]{:S(2)}) async-start(s8[8388608]{0:T(1024)(128)(4,1)} %bitcast.124), calls=%async_computation.4 | async-start | bytes 8388608
  122.9 11.2 %collective-permute-start.11 = (bf16[4,2,256,512]{3,2,1,0:T(8,128)(2,1)S(1)}, bf16[4,2,256,512]{3,2,1,0:T(8,128)(2,1)S(1)}, u32[]{:S(2)}, u32[]{:S(2)}) collective-permute-start(bf16[4,2,256,512]{3,2,1,0:T(8,128)(2,1)S(1)} %pad_maximum_fusion), channel_id=1, source_target_pairs={{0,1},{1,0},{2,3},{3,2},{4,5},{5,4},{6,7},{7,6},{8,9},{9,8},{10,11... | collective-permute-start | bytes 6291464 | tf_op jit(solution)/shard_map/ppermute | solution.py:23
  129.6 4.5 %slice-start.1 = ((s8[8388608]{0:T(1024)(128)(4,1)}), s8[4194304]{0:T(1024)(128)(4,1)S(1)}, s32[]{:S(2)}) async-start(s8[8388608]{0:T(1024)(128)(4,1)} %bitcast.124), calls=%async_computation.5 | async-start | bytes 8388608
  167.7 1.0 copy-start.5
  196.5 6.8 %copy-start.4 = (f32[2,256,512]{2,1,0:T(8,128)S(1)}, f32[2,256,512]{2,1,0:T(8,128)}, u32[]{:S(2)}) copy-start(f32[2,256,512]{2,1,0:T(8,128)} %copy-done.3) | copy-start | bytes 3145732
  196.6 6.8 %copy-start.7 = (bf16[256,512]{1,0:T(8,128)(2,1)S(1)}, bf16[256,512]{1,0:T(8,128)(2,1)}, u32[]{:S(2)}) copy-start(bf16[256,512]{1,0:T(8,128)(2,1)} %copy-done.6) | copy-start | bytes 786436
  199.4 24.0 %all-to-all-start.3 = ((f32[128,1,2052]{2,1,0:T(1,128)}), f32[128,1,2052]{2,1,0:T(1,128)S(1)}, u32[]{:S(2)}, u32[]{:S(2)}) async-start(f32[128,1,2052]{2,1,0:T(1,128)} %broadcast_in_dim.21), calls=%async_computation.3 | async-start | bytes 2228224 | tf_op jit(solution)/shard_map/all_to_all | solution.py:128
where the time goes:
time: 232 us; the launch traced here: 231 us
  waiting for transfers between devices  71.6 us (31%)
  blocking collectives  49.3 us (21%)
  starting transfers between devices  35 us (15%)
  matrix products  25.7 us (11%)
  Pallas kernels  21 us (9%)
  local copies, waits for them, and re-layouts  15 us (6%)
  other arithmetic  11.9 us (5%)
    ppermute x12, waiting for transfers between devices, col_send(): return lax.ppermute(x, 'col', [(c, move(c)) for c in range(n)])  40.9 us
    all_to_all x1, blocking collectives, scatter_sum_by_a2a(): got = lax.all_to_all(parts, axis_name, 0, 0, tiled=False)  28.9 us
    ppermute x12, starting transfers between devices, col_send(): return lax.ppermute(x, 'col', [(c, move(c)) for c in range(n)])  24.1 us
    pallas_call x2, Pallas kernels, place_rows(): pl.pallas_call(functools.partial(place_kernel, row_offset), grid_spec=plt...  21 us
    all_to_all x1, blocking collectives, all_sum_by_a2a(): lax.all_to_all(parts.astype(jnp.bfloat16), axis_names, 0, 0, tiled=False)  20.4 us
    all_to_all x1, waiting for transfers between devices, all_sum_by_a2a(): lax.all_to_all(jnp.broadcast_to(mine[None], parts.shape), axis_names, 0,...  18 us
    all_to_all x1, waiting for transfers between devices, gather_by_a2a(): lax.all_to_all(spread, axis_name, 0, 0, tiled=False)  12.6 us
    dot_general x1, matrix products, on_device_body(): jnp.dot(dense_other, gathered, preferred_element_type=jnp.float32)  7.01 us
  transfers between devices with their start and end apart: 14, of which 9 were waited for; matrix products, arithmetic and copies ran while one was open for 6% of the time, Pallas kernels for 9%

commit v1 on v0

--- a/solution.py
+++ b/solution.py
@@ -57,7 +57,7 @@
     return quad.reshape(rows), col_send(quad, n, lambda c: c ^ 1).reshape(rows)
 
 
-def place_kernel(row_offset, slot_ref, adj_ref, dense_ref, dense_t_ref):
+def place_kernel(row_offset, slot_ref, adj_ref, dense_ref):
     row = pl.program_id(0) + row_offset
     col_total = dense_ref.shape[1] // adj_ref.shape[-1]
     size = adj_ref.shape[-1]
@@ -66,7 +66,6 @@
         tile = adj_ref[jnp.maximum(slot, 0)]
         tile = jnp.where(slot >= 0, tile, jnp.zeros_like(tile))
         dense_ref[:, col * size : (col + 1) * size] = tile
-        dense_t_ref[col * size : (col + 1) * size, :] = tile.T
 
 
 def place_rows(slot_of, tile_data, row_offset, row_count, col_total):
@@ -77,20 +76,14 @@
             num_scalar_prefetch=1,
             grid=(row_count,),
             in_specs=[pl.BlockSpec((slot_total, size, size), lambda r, slots: (0, 0, 0))],
-            out_specs=[
-                pl.BlockSpec((size, col_total * size), lambda r, slots: (r, 0)),
-                pl.BlockSpec((col_total * size, size), lambda r, slots: (0, r)),
-            ],
+            out_specs=pl.BlockSpec((size, col_total * size), lambda r, slots: (r, 0)),
         ),
-        out_shape=[
-            jax.ShapeDtypeStruct((row_count * size, col_total * size), tile_data.dtype),
-            jax.ShapeDtypeStruct((col_total * size, row_count * size), tile_data.dtype),
-        ],
+        out_shape=jax.ShapeDtypeStruct((row_count * size, col_total * size), tile_data.dtype),
         compiler_params=pltpu.CompilerParams(vmem_limit_bytes=48 * 1024 * 1024),
         cost_estimate=pl.CostEstimate(
             flops=0,
             transcendentals=0,
-            bytes_accessed=slot_total * size * size * 2 + 2 * row_count * col_total * size * size * 2,
+            bytes_accessed=slot_total * size * size * 2 + row_count * col_total * size * size * 2,
         ),
     )(slot_of, tile_data)
 
@@ -104,9 +97,9 @@
         jnp.where(pair_range[:, None] == pair_of[None, :], slot_range[None, :], -1), axis=1
     )
     half = row_total // 2
-    mine, mine_t = place_rows(slot_of, tile_data, 0, half, col_total)
-    other, other_t = place_rows(slot_of, tile_data, half, half, col_total)
-    return mine, other, mine_t, other_t
+    mine = place_rows(slot_of, tile_data, 0, half, col_total)
+    other = place_rows(slot_of, tile_data, half, half, col_total)
+    return mine, other
 
 
 def gather_by_a2a(x, axis_name, n):
@@ -123,8 +116,8 @@
 def all_sum_by_a2a(x, axis_names, n, scale):
     pad = (-x.shape[0]) % n
     parts = jnp.pad(x, (0, pad)).reshape(n, -1)
-    got = lax.all_to_all(parts.astype(jnp.bfloat16), axis_names, 0, 0, tiled=False)
-    mine = jnp.sum(got.astype(jnp.float32), axis=0) * scale
+    got = lax.all_to_all(parts, axis_names, 0, 0, tiled=False)
+    mine = jnp.sum(got, axis=0) * scale
     back = lax.all_to_all(jnp.broadcast_to(mine[None], parts.shape), axis_names, 0, 0, tiled=False)
     return back.reshape(-1)[: x.shape[0]]
 
@@ -154,7 +147,7 @@
 
     me_col = lax.axis_index("col")
     rel_rows = relative_col(row_ids // own_blocks, me_col) * own_blocks + row_ids % own_blocks
-    dense_mine, dense_other, dense_t_mine, dense_t_other = dense_blocks(tile_data, rel_rows, col_ids, in_count, row_total, col_total)
+    dense_mine, dense_other = dense_blocks(tile_data, rel_rows, col_ids, in_count, row_total, col_total)
 
     projected = jnp.dot(features, weights, preferred_element_type=jnp.float32).astype(jnp.bfloat16)
     gathered = gather_by_a2a(projected, "row", n_row)
@@ -176,9 +169,13 @@
     activated = jax.nn.silu(shifted).astype(jnp.bfloat16)
     bias_part = jnp.sum(slope_own.astype(jnp.float32), axis=0)
     cols_mine = lax.optimization_barrier(
-        jnp.dot(dense_t_mine, slope_mine, preferred_element_type=jnp.float32)
-    )
-    partial_cols = cols_mine + jnp.dot(dense_t_other, slope_other, preferred_element_type=jnp.float32)
+        lax.dot_general(
+            dense_mine, slope_mine, (((0,), (0,)), ((), ())), preferred_element_type=jnp.float32
+        )
+    )
+    partial_cols = cols_mine + lax.dot_general(
+        dense_other, slope_other, (((0,), (0,)), ((), ())), preferred_element_type=jnp.float32
+    )
     back = scatter_sum_by_a2a(partial_cols, "row", n_row, jnp.bfloat16).astype(jnp.bfloat16)
     grad_input = lax.dot_general(
         back, weights, (((1,), (1,)), ((), ())), preferred_element_type=jnp.float32

time: 232 us -> 230 us (level)
  waiting for transfers between devices: 71.6 us -> 77.1 us
  blocking collectives: 49.3 us -> 54.6 us
  other arithmetic: 11.9 us -> 6.88 us
  Pallas kernels: 21 us -> 17 us
  starting transfers between devices: 35 us -> 32.4 us
    all_to_all x1, blocking collectives: 20.4 us -> 25.7 us  [all_sum_by_a2a(): got = lax.all_to_all(parts, axis_names, 0, 0, tiled=False)]
    convert_element_type x2 -> x0, other arithmetic: 5.17 us -> none  [the longest x1 4.31 us: all_sum_by_a2a(): parts.astype(jnp.bfloat16)]
    pallas_call x2, Pallas kernels: 21 us -> 17 us  [place_rows(): pl.pallas_call(functools.partial(place_kernel, row_offset), grid_spec=plt...]
    ppermute x12, starting transfers between devices: 24.1 us -> 21.4 us  [col_send(): return lax.ppermute(x, 'col', [(c, move(c)) for c in range(n)])]
    ppermute x12, waiting for transfers between devices: 40.9 us -> 43.5 us  [col_send(): return lax.ppermute(x, 'col', [(c, move(c)) for c in range(n)])]
    unnamed x35 -> x25, local copies, waits for them, and re-layouts: 5.29 us -> 4.1 us
  transfers between devices with their start and end apart: 14 -> 14, of which waited for: 9 -> 10; matrix products, arithmetic and copies ran while one was open for 6% -> 6% of each run, Pallas kernels for 9% -> 7%
where the time goes in v1:
time: 230 us
  waiting for transfers between devices  77.1 us (34%)
  blocking collectives  54.6 us (24%)
  starting transfers between devices  32.4 us (14%)
  matrix products  25.8 us (11%)
  Pallas kernels  17 us (7%)
  local copies, waits for them, and re-layouts  14.4 us (6%)
  other arithmetic  6.88 us (3%)
    ppermute x12, waiting for transfers between devices, col_send(): return lax.ppermute(x, 'col', [(c, move(c)) for c in range(n)])  43.5 us
    all_to_all x1, blocking collectives, scatter_sum_by_a2a(): got = lax.all_to_all(parts, axis_name, 0, 0, tiled=False)  28.9 us
    all_to_all x1, blocking collectives, all_sum_by_a2a(): got = lax.all_to_all(parts, axis_names, 0, 0, tiled=False)  25.7 us
    ppermute x12, starting transfers between devices, col_send(): return lax.ppermute(x, 'col', [(c, move(c)) for c in range(n)])  21.4 us
    all_to_all x1, waiting for transfers between devices, all_sum_by_a2a(): lax.all_to_all(jnp.broadcast_to(mine[None], parts.shape), axis_names, 0,...  18.9 us
    pallas_call x2, Pallas kernels, place_rows(): pl.pallas_call(functools.partial(place_kernel, row_offset), grid_spec=plt...  17 us
    all_to_all x1, waiting for transfers between devices, gather_by_a2a(): lax.all_to_all(spread, axis_name, 0, 0, tiled=False)  14.7 us
    dot_general x1, matrix products, on_device_body(): jnp.dot(dense_other, gathered, preferred_element_type=jnp.float32)  7.01 us
  transfers between devices with their start and end apart: 14, of which 10 were waited for; matrix products, arithmetic and copies ran while one was open for 6% of the time, Pallas kernels for 7%

profile of v1, /device:TPU:1, one launch (start us, length us, event | category | flops | bytes accessed | tf_op | source)
XLA Modules:
  0.0 229.8 jit_solution(9547638520714962659)
XLA Ops:
  0.6 0.0 copy-start
  0.6 1.0 copy-done
  1.7 1.2 convolution_convert_fusion.1
  2.9 1.6 broadcast_in_dim.20
  4.5 6.9 %all-to-all-start = ((bf16[8,256,512]{2,1,0:T(8,128)(2,1)}), bf16[8,256,512]{2,1,0:T(8,128)(2,1)S(1)}, u32[]{:S(2)}, u32[]{:S(2)}) async-start(bf16[8,256,512]{2,1,0:T(8,128)(2,1)} %broadcast_in_dim.20), calls=%async_computation | async-start | bytes 4194304 | tf_op jit(solution)/shard_map/all_to_all | solution.py:107
  12.1 0.1 select_reduce_fusion.slot_ref
  12.3 0.0 copy-start.1
  12.3 2.2 copy-done.1
  14.5 8.5 %shard_map.112 = bf16[2048,2048]{1,0:T(8,128)(2,1)} custom-call(s32[512]{0:T(512)S(1)} %select_reduce_fusion.slot_ref, bf16[128,128,128]{2,1,0:T(8,128)(2,1)S(1)} %bitcast.109), custom_call_target="tpu_custom_call" | custom-call | bytes 12582912 | tf_op jit(solution)/shard_map/pallas_call | solution.py:73
  22.9 14.7 %all-to-all-done = bf16[8,256,512]{2,1,0:T(8,128)(2,1)S(1)} async-done(((bf16[8,256,512]{2,1,0:T(8,128)(2,1)}), bf16[8,256,512]{2,1,0:T(8,128)(2,1)S(1)}, u32[]{:S(2)}, u32[]{:S(2)}) %all-to-all-start) | async-done | bytes 2097184 | tf_op jit(solution)/shard_map/all_to_all | solution.py:107
  37.6 7.0 %fusion.23 = f32[4,2,256,512]{3,2,1,0:T(8,128)S(1)} fusion(bf16[4,2,256,2048]{3,2,1,0:T(8,128)(2,1)} %bitcast.111, bf16[2048,512,1,1]{1,0,3,2:T(8,128)(2,1)S(1)} %bitcast.119), kind=kOutput, calls=%fused_computation.73 | convolution fusion | flops 4294967296 | bytes 14680064 | tf_op jit(solution)/shard_map/dot_general | solution.py:154
  44.6 0.9 collective-permute-start
  45.5 8.6 %shard_map.111 = bf16[2048,2048]{1,0:T(8,128)(2,1)} custom-call(s32[512]{0:T(512)S(1)} %select_reduce_fusion.slot_ref, bf16[128,128,128]{2,1,0:T(8,128)(2,1)S(1)} %bitcast.110), custom_call_target="tpu_custom_call" | custom-call | bytes 12582912 | tf_op jit(solution)/shard_map/pallas_call | solution.py:73
  54.1 6.8 %fusion.22 = f32[2048,512]{1,0:T(8,128)S(1)} fusion(bf16[2048,2048]{1,0:T(8,128)(2,1)} %shard_map.111, bf16[2048,512]{1,0:T(8,128)(2,1)S(1)} %bitcast.120), kind=kOutput, calls=%fused_computation.72 | convolution fusion | flops 4294967296 | bytes 14680064 | tf_op jit(solution)/shard_map/dot_general | solution.py:156
  60.9 1.1 fusion.21
  62.0 0.1 slice_bitcast_fusion.9
  62.1 1.4 collective-permute-start.1
  63.5 1.5 collective-permute-start.3
  65.0 6.4 %collective-permute-done.1 = bf16[256,512]{1,0:T(8,128)(2,1)S(1)} collective-permute-done((bf16[256,512]{1,0:T(8,128)(2,1)S(1)}, bf16[256,512]{1,0:T(8,128)(2,1)S(1)}, u32[]{:S(2)}, u32[]{:S(2)}) %collective-permute-start.1) | collective-permute-done | bytes 262176 | tf_op jit(solution)/shard_map/ppermute | solution.py:23
  71.4 0.2 fusion.8
  71.6 0.1 pad_maximum_fusion.3
  71.6 2.6 %collective-permute-start.4 = (bf16[2,256,512]{2,1,0:T(8,128)(2,1)S(1)}, bf16[2,256,512]{2,1,0:T(8,128)(2,1)S(1)}, u32[]{:S(2)}, u32[]{:S(2)}) collective-permute-start(bf16[2,256,512]{2,1,0:T(8,128)(2,1)S(1)} %pad_maximum_fusion.3), channel_id=1, source_target_pairs={{0,12},{1,13},{2,14},{3,15},{4,0},{5,1},{6,2},{7,3},{8,4},{9,5},{1... | collective-permute-start | bytes 1572872 | tf_op jit(solution)/shard_map/ppermute | solution.py:23
  74.2 0.1 pad_maximum_fusion.2
  74.3 0.1 collective-permute-start.2
  74.4 10.1 %collective-permute-done.4 = bf16[2,256,512]{2,1,0:T(8,128)(2,1)S(1)} collective-permute-done((bf16[2,256,512]{2,1,0:T(8,128)(2,1)S(1)}, bf16[2,256,512]{2,1,0:T(8,128)(2,1)S(1)}, u32[]{:S(2)}, u32[]{:S(2)}) %collective-permute-start.4) | collective-permute-done | bytes 524320 | tf_op jit(solution)/shard_map/ppermute | solution.py:23
  84.5 3.3 %collective-permute-done.2 = bf16[2,256,512]{2,1,0:T(8,128)(2,1)S(1)} collective-permute-done((bf16[2,256,512]{2,1,0:T(8,128)(2,1)S(1)}, bf16[2,256,512]{2,1,0:T(8,128)(2,1)S(1)}, u32[]{:S(2)}, u32[]{:S(2)}) %collective-permute-start.2) | collective-permute-done | bytes 524320 | tf_op jit(solution)/shard_map/ppermute | solution.py:23
  87.8 0.2 fusion.1
  88.1 2.5 %collective-permute-start.5 = (bf16[256,512]{1,0:T(8,128)(2,1)S(1)}, bf16[256,512]{1,0:T(8,128)(2,1)S(1)}, u32[]{:S(2)}, u32[]{:S(2)}) collective-permute-start(bf16[256,512]{1,0:T(8,128)(2,1)S(1)} %fusion.10), channel_id=1, source_target_pairs={{0,2},{1,3},{2,0},{3,1},{4,6},{5,7},{6,4},{7,5},{8,10},{9,11},{10,... | collective-permute-start | bytes 786440 | tf_op jit(solution)/shard_map/ppermute | solution.py:23
  90.5 4.9 %collective-permute-done.5 = bf16[256,512]{1,0:T(8,128)(2,1)S(1)} collective-permute-done((bf16[256,512]{1,0:T(8,128)(2,1)S(1)}, bf16[256,512]{1,0:T(8,128)(2,1)S(1)}, u32[]{:S(2)}, u32[]{:S(2)}) %collective-permute-start.5) | collective-permute-done | bytes 262176 | tf_op jit(solution)/shard_map/ppermute | solution.py:23
  95.4 1.0 convert_reduce_fusion
  96.4 2.3 %collective-permute-start.6 = (bf16[256,512]{1,0:T(8,128)(2,1)S(1)}, bf16[256,512]{1,0:T(8,128)(2,1)S(1)}, u32[]{:S(2)}, u32[]{:S(2)}) collective-permute-start(bf16[256,512]{1,0:T(8,128)(2,1)S(1)} %get-tuple-element.5), channel_id=1, source_target_pairs={{0,2},{1,3},{2,0},{3,1},{4,6},{5,7},{6,4},{7,5},{8,10},{9,11},{10,... | collective-permute-start | bytes 786440 | tf_op jit(solution)/shard_map/ppermute | solution.py:23
  98.7 4.4 %collective-permute-done.6 = bf16[256,512]{1,0:T(8,128)(2,1)S(1)} collective-permute-done((bf16[256,512]{1,0:T(8,128)(2,1)S(1)}, bf16[256,512]{1,0:T(8,128)(2,1)S(1)}, u32[]{:S(2)}, u32[]{:S(2)}) %collective-permute-start.6) | collective-permute-done | bytes 262176 | tf_op jit(solution)/shard_map/ppermute | solution.py:23
  103.1 0.1 fusion.20
  103.2 0.5 collective-permute-start.7
  103.7 1.0 collective-permute-start.9
  104.7 7.9 %collective-permute-done.7 = bf16[2,256,512]{2,1,0:T(8,128)(2,1)S(1)} collective-permute-done((bf16[2,256,512]{2,1,0:T(8,128)(2,1)S(1)}, bf16[2,256,512]{2,1,0:T(8,128)(2,1)S(1)}, u32[]{:S(2)}, u32[]{:S(2)}) %collective-permute-start.7) | collective-permute-done | bytes 524320 | tf_op jit(solution)/shard_map/ppermute | solution.py:23
  112.6 2.0 collective-permute-start.8
  114.6 0.1 collective-permute-start.10
  114.7 5.0 %collective-permute-done.8 = bf16[256,512]{1,0:T(8,128)(2,1)S(1)} collective-permute-done((bf16[256,512]{1,0:T(8,128)(2,1)S(1)}, bf16[256,512]{1,0:T(8,128)(2,1)S(1)}, u32[]{:S(2)}, u32[]{:S(2)}) %collective-permute-start.8) | collective-permute-done | bytes 262176 | tf_op jit(solution)/shard_map/ppermute | solution.py:23
  119.7 1.6 collective-permute-done.10
  121.3 0.1 maximum_bitcast_fusion
  121.4 0.3 pad_maximum_fusion
  121.7 6.5 %collective-permute-start.11 = (bf16[4,2,256,512]{3,2,1,0:T(8,128)(2,1)S(1)}, bf16[4,2,256,512]{3,2,1,0:T(8,128)(2,1)S(1)}, u32[]{:S(2)}, u32[]{:S(2)}) collective-permute-start(bf16[4,2,256,512]{3,2,1,0:T(8,128)(2,1)S(1)} %pad_maximum_fusion), channel_id=1, source_target_pairs={{0,1},{1,0},{2,3},{3,2},{4,5},{5,4},{6,7},{7,6},{8,9},{9,8},{10,11... | collective-permute-start | bytes 6291464 | tf_op jit(solution)/shard_map/ppermute | solution.py:23
  128.2 4.6 %fusion.24 = f32[2048,512]{1,0:T(8,128)S(1)} fusion(bf16[2048,2048]{1,0:T(8,128)(2,1)S(1)} %bitcast.115, bf16[2048,512]{1,0:T(8,128)(2,1)S(1)} %bitcast.121), kind=kOutput, calls=%fused_computation.74 | convolution fusion | flops 4294967296 | bytes 14680064 | tf_op jit(solution)/shard_map/dot_general | solution.py:172
  132.8 4.8 %add_convert_fusion = bf16[2048,512]{1,0:T(8,128)(2,1)S(1)} fusion(f32[2048,512]{1,0:T(8,128)S(1)} %fusion.24, bf16[2048,2048]{1,0:T(8,128)(2,1)S(1)} %bitcast.113, bf16[2048,512]{1,0:T(8,128)(2,1)S(1)} %bitcast.129), kind=kOutput, calls=%fused_computation | convolution fusion | flops 4297064448 | bytes 16777216 | tf_op jit(solution)/shard_map/dot_general | solution.py:176
  137.6 28.9 %all_to_all.26 = bf16[8,256,512]{2,1,0:T(8,128)(2,1)S(1)} all-to-all(bf16[8,256,512]{2,1,0:T(8,128)(2,1)S(1)} %bitcast.122), channel_id=1, replica_groups=mesh['row'=8,'col'=16] {'row'}, dimensions={0} | all-to-all | bytes 4194304 | tf_op jit(solution)/shard_map/all_to_all | solution.py:112
  166.4 0.4 reduce_sum.30
  166.8 0.6 copy-done.3
  167.4 0.3 convolution_bitcast_fusion
  167.7 0.3 copy.15
  168.0 0.3 copy.18
  168.3 0.1 pad_maximum_fusion.1
  168.4 1.5 all_to_all.21
  169.9 25.7 %all_to_all.27 = f32[128,1,2052]{2,1,0:T(1,128)S(1)} all-to-all(f32[128,1,2052]{2,1,0:T(1,128)S(1)} %all_to_all.21), channel_id=1, replica_groups=mesh['row'=8,'col'=16] {'row','col'}, dimensions={0} | all-to-all | bytes 2101248 | tf_op jit(solution)/shard_map/all_to_all | solution.py:119
  195.6 0.7 reduce_sum.32
  196.3 1.6 broadcast_in_dim.21
  197.9 4.1 %all-to-all-start.3 = ((f32[128,1,2052]{2,1,0:T(1,128)}), f32[128,1,2052]{2,1,0:T(1,128)S(1)}, u32[]{:S(2)}, u32[]{:S(2)}) async-start(f32[128,1,2052]{2,1,0:T(1,128)} %broadcast_in_dim.21), calls=%async_computation.3 | async-start | bytes 2228224 | tf_op jit(solution)/shard_map/all_to_all | solution.py:121
  202.0 1.0 convolution_convert_fusion
  203.0 18.9 %all-to-all-done.3 = f32[128,1,2052]{2,1,0:T(1,128)S(1)} async-done(((f32[128,1,2052]{2,1,0:T(1,128)}), f32[128,1,2052]{2,1,0:T(1,128)S(1)}, u32[]{:S(2)}, u32[]{:S(2)}) %all-to-all-start.3) | async-done | bytes 1050656 | tf_op jit(solution)/shard_map/all_to_all | solution.py:121
  221.9 2.7 %reduce.2 = f32[128,2052]{1,0:T(8,128)S(1)} reduce(f32[128,1,2052]{2,1,0:T(1,128)S(1)} %all-to-all-done.3, f32[]{:T(128)} %constant.115), dimensions={1}, to_apply=%all_to_all.20.reduce_sub_computation | reduce | bytes 2101252 | tf_op jit(solution)/shard_map/all_to_all | solution.py:121
  224.6 1.8 reshape.196
  226.4 1.1 slice.58
  227.5 1.3 slice.73
  228.7 1.0 slice.72
  (30 shorter events, 0.2 us)
Async XLA Ops:
  0.6 1.0 copy-start
  4.5 7.6 %copy-start.6 = (s32[1,1,128]{2,1,0:T(1,128)S(1)}, s32[1,1,128]{2,1,0:T(1,128)}, u32[]{:S(2)}) copy-start(s32[1,1,128]{2,1,0:T(1,128)} %param.14) | copy-start | bytes 1540
  4.5 7.6 %copy-start.7 = (s32[1,1,128]{2,1,0:T(1,128)S(1)}, s32[1,1,128]{2,1,0:T(1,128)}, u32[]{:S(2)}) copy-start(s32[1,1,128]{2,1,0:T(1,128)} %param.13) | copy-start | bytes 1540
  4.5 33.1 %all-to-all-start = ((bf16[8,256,512]{2,1,0:T(8,128)(2,1)}), bf16[8,256,512]{2,1,0:T(8,128)(2,1)S(1)}, u32[]{:S(2)}, u32[]{:S(2)}) async-start(bf16[8,256,512]{2,1,0:T(8,128)(2,1)} %broadcast_in_dim.20), calls=%async_computation | async-start | bytes 4194304 | tf_op jit(solution)/shard_map/all_to_all | solution.py:107
  12.3 2.2 copy-start.1
  37.6 7.9 %copy-start.2 = (bf16[1,1,128,128,128]{4,3,2,1,0:T(8,128)(2,1)S(1)}, bf16[1,1,128,128,128]{4,3,2,1,0:T(8,128)(2,1)}, u32[]{:S(2)}) copy-start(bf16[1,1,128,128,128]{4,3,2,1,0:T(8,128)(2,1)} %param.12) | copy-start | bytes 12582916
  44.6 16.3 %collective-permute-start = (f32[4,2,256,512]{3,2,1,0:T(8,128)S(1)}, f32[4,2,256,512]{3,2,1,0:T(8,128)S(1)}, u32[]{:S(2)}, u32[]{:S(2)}) collective-permute-start(f32[4,2,256,512]{3,2,1,0:T(8,128)S(1)} %fusion.23), channel_id=1, source_target_pairs={{0,1},{1,0},{2,3},{3,2},{4,5},{5,4},{6,7},{7,6},{8,9},{9,8},{10,11... | collective-permute-start | bytes 12582920 | tf_op jit(solution)/shard_map/ppermute | solution.py:23
  62.1 9.3 %collective-permute-start.1 = (bf16[256,512]{1,0:T(8,128)(2,1)S(1)}, bf16[256,512]{1,0:T(8,128)(2,1)S(1)}, u32[]{:S(2)}, u32[]{:S(2)}) collective-permute-start(bf16[256,512]{1,0:T(8,128)(2,1)S(1)} %get-tuple-element.10), channel_id=1, source_target_pairs={{0,4},{1,5},{2,6},{3,7},{4,8},{5,9},{6,10},{7,11},{8,12},{9,13},{1... | collective-permute-start | bytes 786440 | tf_op jit(solution)/shard_map/ppermute | solution.py:23
  63.5 7.9 %collective-permute-start.3 = (bf16[256,512]{1,0:T(8,128)(2,1)S(1)}, bf16[256,512]{1,0:T(8,128)(2,1)S(1)}, u32[]{:S(2)}, u32[]{:S(2)}) collective-permute-start(bf16[256,512]{1,0:T(8,128)(2,1)S(1)} %get-tuple-element.11), channel_id=1, source_target_pairs={{0,12},{1,13},{2,14},{3,15},{4,0},{5,1},{6,2},{7,3},{8,4},{9,5},{1... | collective-permute-start | bytes 786440 | tf_op jit(solution)/shard_map/ppermute | solution.py:23
  71.6 56.6 %slice-start.2 = ((s8[8388608]{0:T(1024)(128)(4,1)}), s8[4194304]{0:T(1024)(128)(4,1)S(1)}, s32[]{:S(2)}) async-start(s8[8388608]{0:T(1024)(128)(4,1)} %bitcast.114), calls=%async_computation.6 | async-start | bytes 8388608
  71.6 12.9 %collective-permute-start.4 = (bf16[2,256,512]{2,1,0:T(8,128)(2,1)S(1)}, bf16[2,256,512]{2,1,0:T(8,128)(2,1)S(1)}, u32[]{:S(2)}, u32[]{:S(2)}) collective-permute-start(bf16[2,256,512]{2,1,0:T(8,128)(2,1)S(1)} %pad_maximum_fusion.3), channel_id=1, source_target_pairs={{0,12},{1,13},{2,14},{3,15},{4,0},{5,1},{6,2},{7,3},{8,4},{9,5},{1... | collective-permute-start | bytes 1572872 | tf_op jit(solution)/shard_map/ppermute | solution.py:23
  74.3 21.1 %copy-start.4 = (bf16[256,512]{1,0:T(8,128)(2,1)S(1)}, bf16[256,512]{1,0:T(8,128)(2,1)}, u32[]{:S(2)}) copy-start(bf16[256,512]{1,0:T(8,128)(2,1)} %param.9) | copy-start | bytes 786436
  74.3 21.1 %copy-start.5 = (f32[512]{0:T(512)S(1)}, f32[512]{0:T(512)}, u32[]{:S(2)}) copy-start(f32[512]{0:T(512)} %param.11) | copy-start | bytes 6148
  74.3 13.5 %collective-permute-start.2 = (bf16[2,256,512]{2,1,0:T(8,128)(2,1)S(1)}, bf16[2,256,512]{2,1,0:T(8,128)(2,1)S(1)}, u32[]{:S(2)}, u32[]{:S(2)}) collective-permute-start(bf16[2,256,512]{2,1,0:T(8,128)(2,1)S(1)} %pad_maximum_fusion.2), channel_id=1, source_target_pairs={{0,4},{1,5},{2,6},{3,7},{4,8},{5,9},{6,10},{7,11},{8,12},{9,13},{1... | collective-permute-start | bytes 1572872 | tf_op jit(solution)/shard_map/ppermute | solution.py:23
  88.1 7.3 %collective-permute-start.5 = (bf16[256,512]{1,0:T(8,128)(2,1)S(1)}, bf16[256,512]{1,0:T(8,128)(2,1)S(1)}, u32[]{:S(2)}, u32[]{:S(2)}) collective-permute-start(bf16[256,512]{1,0:T(8,128)(2,1)S(1)} %fusion.10), channel_id=1, source_target_pairs={{0,2},{1,3},{2,0},{3,1},{4,6},{5,7},{6,4},{7,5},{8,10},{9,11},{10,... | collective-permute-start | bytes 786440 | tf_op jit(solution)/shard_map/ppermute | solution.py:23
  96.4 6.7 %collective-permute-start.6 = (bf16[256,512]{1,0:T(8,128)(2,1)S(1)}, bf16[256,512]{1,0:T(8,128)(2,1)S(1)}, u32[]{:S(2)}, u32[]{:S(2)}) collective-permute-start(bf16[256,512]{1,0:T(8,128)(2,1)S(1)} %get-tuple-element.5), channel_id=1, source_target_pairs={{0,2},{1,3},{2,0},{3,1},{4,6},{5,7},{6,4},{7,5},{8,10},{9,11},{10,... | collective-permute-start | bytes 786440 | tf_op jit(solution)/shard_map/ppermute | solution.py:23
  103.1 25.1 %slice-start.3 = ((s8[8388608]{0:T(1024)(128)(4,1)}), s8[4194304]{0:T(1024)(128)(4,1)S(1)}, s32[]{:S(2)}) async-start(s8[8388608]{0:T(1024)(128)(4,1)} %bitcast.114), calls=%async_computation.7 | async-start | bytes 8388608
  103.2 9.4 %collective-permute-start.7 = (bf16[2,256,512]{2,1,0:T(8,128)(2,1)S(1)}, bf16[2,256,512]{2,1,0:T(8,128)(2,1)S(1)}, u32[]{:S(2)}, u32[]{:S(2)}) collective-permute-start(bf16[2,256,512]{2,1,0:T(8,128)(2,1)S(1)} %get-tuple-element.16), channel_id=1, source_target_pairs={{0,12},{1,13},{2,14},{3,15},{4,0},{5,1},{6,2},{7,3},{8,4},{9,5},{1... | collective-permute-start | bytes 1572872 | tf_op jit(solution)/shard_map/ppermute | solution.py:23
  103.7 10.9 %collective-permute-start.9 = (bf16[2,256,512]{2,1,0:T(8,128)(2,1)S(1)}, bf16[2,256,512]{2,1,0:T(8,128)(2,1)S(1)}, u32[]{:S(2)}, u32[]{:S(2)}) collective-permute-start(bf16[2,256,512]{2,1,0:T(8,128)(2,1)S(1)} %get-tuple-element.16), channel_id=1, source_target_pairs={{0,4},{1,5},{2,6},{3,7},{4,8},{5,9},{6,10},{7,11},{8,12},{9,13},{1... | collective-permute-start | bytes 1572872 | tf_op jit(solution)/shard_map/ppermute | solution.py:23
  112.6 7.1 %collective-permute-start.8 = (bf16[256,512]{1,0:T(8,128)(2,1)S(1)}, bf16[256,512]{1,0:T(8,128)(2,1)S(1)}, u32[]{:S(2)}, u32[]{:S(2)}) collective-permute-start(bf16[256,512]{1,0:T(8,128)(2,1)S(1)} %slice_bitcast_fusion.5), channel_id=1, source_target_pairs={{0,12},{1,13},{2,14},{3,15},{4,0},{5,1},{6,2},{7,3},{8,4},{9,5},{1... | collective-permute-start | bytes 786440 | tf_op jit(solution)/shard_map/ppermute | solution.py:23
  114.6 6.7 %collective-permute-start.10 = (bf16[256,512]{1,0:T(8,128)(2,1)S(1)}, bf16[256,512]{1,0:T(8,128)(2,1)S(1)}, u32[]{:S(2)}, u32[]{:S(2)}) collective-permute-start(bf16[256,512]{1,0:T(8,128)(2,1)S(1)} %slice_bitcast_fusion.4), channel_id=1, source_target_pairs={{0,4},{1,5},{2,6},{3,7},{4,8},{5,9},{6,10},{7,11},{8,12},{9,13},{1... | collective-permute-start | bytes 786440 | tf_op jit(solution)/shard_map/ppermute | solution.py:23
  121.4 11.4 %slice-start = ((s8[8388608]{0:T(1024)(128)(4,1)}), s8[4194304]{0:T(1024)(128)(4,1)S(1)}, s32[]{:S(2)}) async-start(s8[8388608]{0:T(1024)(128)(4,1)} %bitcast.112), calls=%async_computation.4 | async-start | bytes 8388608
  121.7 11.1 %collective-permute-start.11 = (bf16[4,2,256,512]{3,2,1,0:T(8,128)(2,1)S(1)}, bf16[4,2,256,512]{3,2,1,0:T(8,128)(2,1)S(1)}, u32[]{:S(2)}, u32[]{:S(2)}) collective-permute-start(bf16[4,2,256,512]{3,2,1,0:T(8,128)(2,1)S(1)} %pad_maximum_fusion), channel_id=1, source_target_pairs={{0,1},{1,0},{2,3},{3,2},{4,5},{5,4},{6,7},{7,6},{8,9},{9,8},{10,11... | collective-permute-start | bytes 6291464 | tf_op jit(solution)/shard_map/ppermute | solution.py:23
  128.2 4.6 %slice-start.1 = ((s8[8388608]{0:T(1024)(128)(4,1)}), s8[4194304]{0:T(1024)(128)(4,1)S(1)}, s32[]{:S(2)}) async-start(s8[8388608]{0:T(1024)(128)(4,1)} %bitcast.112), calls=%async_computation.5 | async-start | bytes 8388608
  166.4 1.0 copy-start.3
  197.9 24.0 %all-to-all-start.3 = ((f32[128,1,2052]{2,1,0:T(1,128)}), f32[128,1,2052]{2,1,0:T(1,128)S(1)}, u32[]{:S(2)}, u32[]{:S(2)}) async-start(f32[128,1,2052]{2,1,0:T(1,128)} %broadcast_in_dim.21), calls=%async_computation.3 | async-start | bytes 2228224 | tf_op jit(solution)/shard_map/all_to_all | solution.py:121
